TPU v7x, 256 devices: a whole 4x4x8 slice. The times are simulated.
256 devices in a mesh: row: 4 (over y), col: 64 (over z, x, core).
Axes of the slice: x: 4, y: 4, z: 8, core: 2. Of those that a mesh axis runs over, the one named last changes fastest.
Arguments:
- tokens: bfloat16 [32768, 4096], P(('row', 'col')), may hold values from -6 to 6
- expert_ids: int32 [32768, 2], P(('row', 'col')), may hold values from 0 to 63, all different within a row; in each aligned block of 128 rows (0 to 127, 128 to 255, ...) at most 5 rows name the same one
- gate_weights: float32 [32768, 2], P(('row', 'col')), may hold values from 0.1 to 1
- w_gate: bfloat16 [64, 4096, 1536], P('col', None, 'row'), may hold values from -0.09375 to 0.09375
- w_up: bfloat16 [64, 4096, 1536], P('col', None, 'row'), may hold values from -0.09375 to 0.09375
- w_down: bfloat16 [64, 1536, 4096], P('col', None, 'row'), may hold values from -0.15625 to 0.15625
Outputs:
- moe_out: bfloat16 [32768, 4096], P(('row', 'col'))
Inputs may be any that keep to these rules, and one draw needn't show every extreme that they name: `expert_ids`: each row names 2 different experts. Among the 128 rows of one device no expert is named by more than 5 rows, and in every draw some expert is named by exactly 5 rows of some device.
All inputs are finite; a program needn't handle non-finite values.
Results may differ from a plain program's by a relative error of at most 0.0058.
Values may be sent and summed in bfloat16 or wider, within the bound.
No kernel may reach another device: no remote copies, remote signals or barrier semaphores. Data moves between devices by JAX's collectives and lax.ppermute only.
A program may use at most 128 MiB of HBM per device.

v0:
```python
import jax
import jax.numpy as jnp
from jax import lax
from jax.sharding import PartitionSpec as P


def local(tokens, expert_ids, gate_weights, w_gate, w_up, w_down):
    token_count, top_count = expert_ids.shape
    width = tokens.shape[1]
    local_count = w_gate.shape[0]
    unit_count = w_gate.shape[2]
    quarter = w_down.shape[2]
    columns = lax.axis_size("col")
    groups = lax.axis_size("row")
    experts = local_count * columns
    capacity = max(2, token_count * top_count * 5 // (4 * experts))
    flat_ids = expert_ids.reshape(-1)
    onehot = (flat_ids[:, None] == jnp.arange(experts, dtype=jnp.int32)[None, :]).astype(jnp.int32)
    earlier = jnp.cumsum(onehot, axis=0) - onehot
    position = jnp.sum(earlier * onehot, axis=1)
    slot_ids = (flat_ids * capacity + position).reshape(token_count, top_count)
    chooser = jnp.any(
        jnp.arange(experts * capacity, dtype=jnp.int32)[:, None, None] == slot_ids[None, :, :],
        axis=2,
    ).astype(jnp.bfloat16)
    outgoing = jnp.dot(chooser, tokens, preferred_element_type=jnp.float32).astype(jnp.bfloat16)
    outgoing = outgoing.reshape(columns, local_count * capacity, width)
    arrived = lax.all_to_all(outgoing, "col", split_axis=0, concat_axis=0, tiled=True)
    block_rows = lax.all_gather(arrived[None], "row", axis=0, tiled=True)
    count = block_rows.shape[0]
    grouped = block_rows.reshape(count, columns, local_count, capacity, width)
    expert = 0
    inputs = grouped[:, :, expert].reshape(-1, width)
    gate_part = jnp.dot(inputs, w_gate[expert], preferred_element_type=jnp.float32)
    up_part = jnp.dot(inputs, w_up[expert], preferred_element_type=jnp.float32)
    hidden = (jax.nn.silu(gate_part) * up_part).astype(jnp.bfloat16)
    outputs = hidden.reshape(count, columns, 1, capacity, unit_count)
    hidden_all = outputs.reshape(count, columns, local_count * capacity, unit_count)
    hidden_split = hidden_all.reshape(groups, columns, local_count, capacity, unit_count)
    piece = lax.all_gather(hidden_split, "row", axis=4, tiled=True)
    count = piece.shape[4]
    expert = 0
    rows = piece[:, :, expert].reshape(-1, count)
    block = w_down[expert]
    parts = [jnp.dot(rows, block, preferred_element_type=jnp.float32)]
    summed = jnp.stack(parts)
    expert_out = summed.astype(jnp.bfloat16).reshape(
        local_count, groups, columns, capacity, quarter
    )
    expert_out = jnp.transpose(expert_out, (1, 2, 0, 3, 4)).reshape(
        groups, columns, local_count * capacity, quarter
    )
    colwise = lax.all_to_all(expert_out, "col", split_axis=1, concat_axis=1, tiled=True)
    home = lax.all_to_all(colwise, "row", split_axis=0, concat_axis=3, tiled=True)
    results = home.reshape(experts * capacity, width)
    shares = gate_weights / jnp.sum(gate_weights, axis=1, keepdims=True)
    picked = results[slot_ids].astype(jnp.float32)
    combined = jnp.sum(shares[:, :, None] * picked, axis=1)
    return combined.astype(jnp.bfloat16)


def solution(mesh):
    placed = (
        P(("row", "col"), None),
        P(("row", "col"), None),
        P(("row", "col"), None),
        P("col", None, "row"),
        P("col", None, "row"),
        P("col", None, "row"),
    )
    return jax.shard_map(
        local, mesh=mesh, in_specs=placed, out_specs=P(("row", "col"), None), check_vma=False
    )
```

profile of v0, /device:TPU:1, one launch (start us, length us, event | category | flops | bytes accessed | tf_op | source)
XLA Modules:
  0.0 528.3 jit_solution(9375818899468450079)
XLA Ops:
  6.5 0.0 copy-start
  6.5 0.0 all-gather.6.cloned.1.call-start
  6.5 0.9 copy.41
  7.5 0.1 eq.43
  7.6 0.1 eq.39
  7.8 0.6 reduce-window.6
  8.4 0.2 slice_reduce_fusion
  8.6 0.1 fusion.10
  8.7 0.1 reduce_sum.31
  8.9 0.1 copy.44
  8.9 0.7 compare_select_fusion
  9.7 3.6 convolution_convert_fusion
  13.3 4.7 reshape.38
  18.0 107.6 %all_to_all.25 = bf16[64,5,4096]{2,1,0:T(8,128)(2,1)S(1)} all-to-all(bf16[64,5,4096]{2,1,0:T(8,128)(2,1)} %reshape.38), channel_id=1, replica_groups=mesh['row'=4,'col'=64] {'col'}, dimensions={0} | all-to-all | bytes 5242880 | tf_op jit(solution)/shard_map/all_to_all | solution.py:28
  125.6 3.2 copy.45
  128.8 0.0 all-gather.6.cloned.1.call-update
  128.8 0.3 all-gather.4.cloned.1.call-start
  129.2 101.0 %all-gather.6.cloned.1.call-done = bf16[256,5,4096]{2,0,1:T(8,128)(2,1)} async-done(((bf16[64,5,4096]{2,0,1:T(8,128)(2,1)}), bf16[256,5,4096]{2,0,1:T(8,128)(2,1)}) %all-gather.6.cloned.1.call-update) | async-done | bytes 10485776 | tf_op jit(solution)/shard_map/all_gather | solution.py:29
  230.2 15.2 %copy.46 = bf16[256,5,4096]{2,1,0:T(8,128)(2,1)} copy(bf16[256,5,4096]{2,0,1:T(8,128)(2,1)} %all-gather.6.cloned.1.call-done) | data formatting | bytes 20971520 | tf_op jit(solution)/shard_map/all_gather | solution.py:29
  245.4 16.8 %reshape_squeeze_reshape.3 = bf16[1280,4096]{1,0:T(8,128)(2,1)} reshape(bf16[256,5,4096]{2,1,0:T(8,128)(2,1)} %copy.46) | data formatting | bytes 20971520 | tf_op jit(solution)/shard_map/reshape;squeeze;reshape | solution.py:33
  262.3 0.0 copy-start.1
  262.3 0.0 copy-start.3
  262.3 9.3 %fusion.2 = f32[1280,384]{1,0:T(8,128)S(1)} fusion(bf16[1280,4096]{1,0:T(8,128)(2,1)} %reshape_squeeze_reshape.3, bf16[1,4096,384]{2,1,0:T(8,128)(2,1)} %param.9), kind=kOutput, calls=%fused_computation.7 | convolution fusion | flops 4026531840 | bytes 15597568 | tf_op jit(solution)/shard_map/dot_general | solution.py:34
  271.6 0.0 copy-done.1
  271.6 0.0 copy-done.3
  271.6 6.9 %fusion.4 = bf16[1280,384]{1,0:T(8,128)(2,1)} fusion(bf16[1280,4096]{1,0:T(8,128)(2,1)S(1)} %copy-done.1, bf16[1,4096,384]{2,1,0:T(8,128)(2,1)S(1)} %copy-done.3, f32[1280,384]{1,0:T(8,128)S(1)} %fusion.2), kind=kOutput, calls=%fused_computation.9 | convolution fusion | flops 4029480960 | bytes 16580608 | tf_op jit(solution)/shard_map/dot_general | solution.py:35
  278.6 3.0 reshape_reshape_reshape.3
  281.5 0.0 all-gather.4.cloned.1.call-update
  281.5 69.4 %all-gather.4.cloned.1.call-done = bf16[4,64,1,5,1536]{4,3,1,0,2:T(8,128)(2,1)} async-done(((bf16[4,64,1,5,384]{4,3,1,0,2:T(8,128)(2,1)}), bf16[4,64,1,5,1536]{4,3,1,0,2:T(8,128)(2,1)}) %all-gather.4.cloned.1.call-update) | async-done | bytes 3932176 | tf_op jit(solution)/shard_map/all_gather | solution.py:40
  351.0 7.6 %reshape_squeeze.3 = bf16[1280,1536]{1,0:T(8,128)(2,1)} reshape(bf16[4,64,1,5,1536]{4,3,1,0,2:T(8,128)(2,1)} %all-gather.4.cloned.1.call-done) | data formatting | bytes 7864320 | tf_op jit(solution)/shard_map/reshape;squeeze | solution.py:43
  358.6 0.0 copy-done
  358.6 7.6 %convolution_convert_fusion.1 = bf16[1280,1024]{1,0:T(8,128)(2,1)} fusion(bf16[1280,1536]{1,0:T(8,128)(2,1)} %reshape_squeeze.3, bf16[1,1536,1024]{2,1,0:T(8,128)(2,1)S(1)} %copy-done), kind=kOutput, calls=%fused_computation.3 | convolution fusion | flops 4027842560 | bytes 9699328 | tf_op jit(solution)/shard_map/dot_general | solution.py:45
  366.2 6.5 %reshape_transpose_reshape.3 = bf16[4,64,5,1024]{3,2,1,0:T(8,128)(2,1)} reshape(bf16[1280,1024]{1,0:T(8,128)(2,1)} %convolution_convert_fusion.1) | data formatting | bytes 5242880 | tf_op jit(solution)/shard_map/reshape;transpose;reshape | solution.py:50
  372.8 7.3 %copy.47 = bf16[4,64,5,1024]{3,0,2,1:T(4,128)(2,1)S(1)} copy(bf16[4,64,5,1024]{3,2,1,0:T(8,128)(2,1)} %reshape_transpose_reshape.3) | data formatting | bytes 5242880 | tf_op jit(solution)/shard_map/reshape;transpose;reshape | solution.py:50
  380.1 73.2 %all_to_all.26 = bf16[4,64,5,1024]{3,0,2,1:T(4,128)(2,1)S(1)} all-to-all(bf16[4,64,5,1024]{3,0,2,1:T(4,128)(2,1)S(1)} %copy.47), channel_id=1, replica_groups=mesh['row'=4,'col'=64] {'col'}, dimensions={1} | all-to-all | bytes 5242880 | tf_op jit(solution)/shard_map/all_to_all | solution.py:53
  453.3 2.3 copy.48
  455.6 0.0 copy-start.2
  455.7 4.8 all-to-all-start.2
  460.5 0.1 copy.50
  460.6 0.1 reshape.42
  460.8 0.0 copy-done.2
  460.8 0.1 copy.40
  460.9 31.4 %all-to-all-done.2 = bf16[4,64,5,1024]{3,1,2,0:T(8,128)(2,1)} async-done(((bf16[4,64,5,1024]{3,1,2,0:T(8,128)(2,1)}), bf16[4,64,5,1024]{3,1,2,0:T(8,128)(2,1)}, u32[]{:S(2)}, u32[]{:S(2)}) %all-to-all-start.2) | async-done | bytes 2621472 | tf_op jit(solution)/shard_map/all_to_all | solution.py:54
  492.3 3.8 copy.49
  496.0 2.6 copy.52
  498.7 7.3 %gather_fusion = bf16[256,4096]{1,0:T(8,128)(2,1)} fusion(bf16[320,4096]{1,0:T(8,128)(2,1)} %bitcast.43, s32[1024]{0:T(1024)S(1)} %pad_clamp_fusion), kind=kCustom, calls=%fused_computation | custom fusion | bytes 4195328 | tf_op jit(solution)/shard_map/gather | solution.py:57
  506.0 5.6 %reshape.52 = f32[128,2,4096]{2,1,0:T(2,128)} reshape(bf16[256,4096]{1,0:T(8,128)(2,1)} %gather_fusion) | data formatting | bytes 6291456 | tf_op jit(solution)/shard_map/convert_element_type | solution.py:57
  511.6 9.6 %multiply_reduce_fusion = bf16[128,4096]{1,0:T(8,128)(2,1)} fusion(f32[128,2,4096]{2,1,0:T(2,128)} %reshape.52, f32[128,2]{1,0:T(8,128)S(1)} %copy.40), kind=kLoop, calls=%fused_computation.2 | loop fusion | flops 1572864 | bytes 5243904 | tf_op jit(solution)/shard_map/reduce_sum | solution.py:58
  (7 shorter events, 0.1 us)
Async XLA Ops:
  6.5 352.1 %copy-start = (bf16[1,1536,1024]{2,1,0:T(8,128)(2,1)S(1)}, bf16[1,1536,1024]{2,1,0:T(8,128)(2,1)}, u32[]{:S(2)}) copy-start(bf16[1,1536,1024]{2,1,0:T(8,128)(2,1)} %param.11) | copy-start | bytes 9437188
  6.5 223.7 %all-gather.6.cloned.1.call-start = ((), (), s32[]{:S(2)}) async-start(), calls=%async_computation.4 | async-start | bytes 13107200 | tf_op jit(solution)/shard_map/all_gather | solution.py:29
  128.8 222.1 %all-gather.4.cloned.1.call-start = ((), (), s32[]{:S(2)}) async-start(), calls=%async_computation.3 | async-start | bytes 7864320 | tf_op jit(solution)/shard_map/all_gather | solution.py:40
  262.3 9.4 %copy-start.1 = (bf16[1280,4096]{1,0:T(8,128)(2,1)S(1)}, bf16[1280,4096]{1,0:T(8,128)(2,1)}, u32[]{:S(2)}) copy-start(bf16[1280,4096]{1,0:T(8,128)(2,1)} %reshape_squeeze_reshape.3) | copy-start | bytes 31457284
  262.3 9.4 %copy-start.3 = (bf16[1,4096,384]{2,1,0:T(8,128)(2,1)S(1)}, bf16[1,4096,384]{2,1,0:T(8,128)(2,1)}, u32[]{:S(2)}) copy-start(bf16[1,4096,384]{2,1,0:T(8,128)(2,1)} %param.10) | copy-start | bytes 9437188
  455.6 5.1 copy-start.2
  455.7 36.6 %all-to-all-start.2 = ((bf16[4,64,5,1024]{3,1,2,0:T(8,128)(2,1)}), bf16[4,64,5,1024]{3,1,2,0:T(8,128)(2,1)}, u32[]{:S(2)}, u32[]{:S(2)}) async-start(bf16[4,64,5,1024]{3,1,2,0:T(8,128)(2,1)} %copy.48), calls=%async_computation.2 | async-start | bytes 5242880 | tf_op jit(solution)/shard_map/all_to_all | solution.py:54
Sparse Core Ops, SparseCore 0:
  128.9 101.2 all-gather.5
  281.7 69.2 all-gather.3
where the time goes:
time: 534 us; the launch traced here: 528 us
  waiting for transfers between devices  202 us (38%)
  blocking collectives  181 us (34%)
  local copies, waits for them, and re-layouts  88.1 us (16%)
  matrix products  27.4 us (5%)
  between operations  13.7 us (3%)
  other arithmetic  11.2 us (2%)
    all_to_all x1, blocking collectives, local(): lax.all_to_all(outgoing, 'col', split_axis=0, concat_axis=0, tiled=True)  108 us
    all_gather x1, waiting for transfers between devices, local(): block_rows = lax.all_gather(arrived[None], 'row', axis=0, tiled=True)  101 us
    all_to_all x1, blocking collectives, local(): lax.all_to_all(expert_out, 'col', split_axis=1, concat_axis=1, tiled=True)  73.2 us
    all_gather x1, waiting for transfers between devices, local(): piece = lax.all_gather(hidden_split, 'row', axis=4, tiled=True)  69.4 us
    all_to_all x1, waiting for transfers between devices, local(): lax.all_to_all(colwise, 'row', split_axis=0, concat_axis=3, tiled=True)  31.4 us
    another operation x1, local copies, waits for them, and re-layouts, local(): inputs = grouped[:, :, expert].reshape(-1, width)  16.8 us
    all_gather x1, local copies, waits for them, and re-layouts, local(): block_rows = lax.all_gather(arrived[None], 'row', axis=0, tiled=True)  15.2 us
    another operation x2, local copies, waits for them, and re-layouts, local(): jnp.transpose(expert_out, (1, 2, 0, 3, 4))  13.9 us
  transfers between devices with their start and end apart: 3, of which 3 were waited for; matrix products, arithmetic and copies ran while one was open for 0% of the time, Pallas kernels for 0%

commit v1 on v0

--- a/solution.py
+++ b/solution.py
@@ -37,7 +37,10 @@
     outputs = hidden.reshape(count, columns, 1, capacity, unit_count)
     hidden_all = outputs.reshape(count, columns, local_count * capacity, unit_count)
     hidden_split = hidden_all.reshape(groups, columns, local_count, capacity, unit_count)
-    piece = lax.all_gather(hidden_split, "row", axis=4, tiled=True)
+    count_2 = lax.axis_size("row")
+    blocks = jnp.stack([hidden_split for _ in range(count_2)])
+    blocks = lax.all_to_all(blocks, "row", split_axis=0, concat_axis=0)
+    piece = jnp.concatenate(blocks, axis=4)
     count = piece.shape[4]
     expert = 0
     rows = piece[:, :, expert].reshape(-1, count)

time: 534 us -> 509 us (0.953)
  waiting for transfers between devices: 202 us -> 133 us
  blocking collectives: 181 us -> 231 us
    all_gather x1 -> x0, waiting for transfers between devices: 69.4 us -> none  [local(): piece = lax.all_gather(hidden_split, 'row', axis=4, tiled=True)]
    all_to_all x0 -> x1, blocking collectives: none -> 49.1 us  [local(): blocks = lax.all_to_all(blocks, 'row', split_axis=0, concat_axis=0)]
    another operation x3 -> x4, local copies, waits for them, and re-layouts: 10.6 us -> 5.23 us  [the longest x3 5.23 us: local(): blocks = jnp.stack([hidden_split for _ in range(count_2)])]
  transfers between devices with their start and end apart: 3 -> 2, of which waited for: 3 -> 2; matrix products, arithmetic and copies ran while one was open for 0% -> 0% of each run, Pallas kernels for 0% -> 0%
where the time goes in v1:
time: 509 us; the launch traced here: 505 us
  blocking collectives  231 us (45%)
  waiting for transfers between devices  133 us (26%)
  local copies, waits for them, and re-layouts  86 us (17%)
  matrix products  25.4 us (5%)
  between operations  13.8 us (3%)
  other arithmetic  11.2 us (2%)
    all_to_all x1, blocking collectives, local(): lax.all_to_all(outgoing, 'col', split_axis=0, concat_axis=0, tiled=True)  108 us
    all_gather x1, waiting for transfers between devices, local(): block_rows = lax.all_gather(arrived[None], 'row', axis=0, tiled=True)  101 us
    all_to_all x1, blocking collectives, local(): lax.all_to_all(expert_out, 'col', split_axis=1, concat_axis=1, tiled=True)  74.4 us
    all_to_all x1, blocking collectives, local(): blocks = lax.all_to_all(blocks, 'row', split_axis=0, concat_axis=0)  49.1 us
    all_to_all x1, waiting for transfers between devices, local(): lax.all_to_all(colwise, 'row', split_axis=0, concat_axis=3, tiled=True)  31.4 us
    another operation x1, local copies, waits for them, and re-layouts, local(): inputs = grouped[:, :, expert].reshape(-1, width)  16.8 us
    all_gather x1, local copies, waits for them, and re-layouts, local(): block_rows = lax.all_gather(arrived[None], 'row', axis=0, tiled=True)  15.2 us
    another operation x2, local copies, waits for them, and re-layouts, local(): jnp.transpose(expert_out, (1, 2, 0, 3, 4))  13.4 us
  transfers between devices with their start and end apart: 2, of which 2 were waited for; matrix products, arithmetic and copies ran while one was open for 0% of the time, Pallas kernels for 0%

profile of v1, /device:TPU:1, one launch (start us, length us, event | category | flops | bytes accessed | tf_op | source)
XLA Modules:
  0.0 505.1 jit_solution(18416693582367651686)
XLA Ops:
  6.5 0.0 copy-start
  6.5 0.0 all-gather.3.cloned.1.call-start
  6.5 0.9 copy.57
  7.5 0.1 eq.43
  7.6 0.1 eq.39
  7.8 0.6 reduce-window.6
  8.4 0.2 slice_reduce_fusion
  8.6 0.1 fusion.10
  8.7 0.1 reduce_sum.31
  8.9 0.1 copy.60
  8.9 0.7 compare_select_fusion
  9.7 3.6 convolution_convert_fusion
  13.3 4.7 reshape.45
  18.0 107.9 %all_to_all.30 = bf16[64,5,4096]{2,1,0:T(8,128)(2,1)S(1)} all-to-all(bf16[64,5,4096]{2,1,0:T(8,128)(2,1)} %reshape.45), channel_id=1, replica_groups=mesh['row'=4,'col'=64] {'col'}, dimensions={0} | all-to-all | bytes 5242880 | tf_op jit(solution)/shard_map/all_to_all | solution.py:28
  125.8 3.2 copy.61
  129.1 0.0 all-gather.3.cloned.1.call-update
  129.1 101.4 %all-gather.3.cloned.1.call-done = bf16[256,5,4096]{2,0,1:T(8,128)(2,1)} async-done(((bf16[64,5,4096]{2,0,1:T(8,128)(2,1)}), bf16[256,5,4096]{2,0,1:T(8,128)(2,1)}) %all-gather.3.cloned.1.call-update) | async-done | bytes 10485776 | tf_op jit(solution)/shard_map/all_gather | solution.py:29
  230.5 15.2 %copy.62 = bf16[256,5,4096]{2,1,0:T(8,128)(2,1)} copy(bf16[256,5,4096]{2,0,1:T(8,128)(2,1)} %all-gather.3.cloned.1.call-done) | data formatting | bytes 20971520 | tf_op jit(solution)/shard_map/all_gather | solution.py:29
  245.7 16.8 %reshape_squeeze_reshape.6 = bf16[1280,4096]{1,0:T(8,128)(2,1)} reshape(bf16[256,5,4096]{2,1,0:T(8,128)(2,1)} %copy.62) | data formatting | bytes 20971520 | tf_op jit(solution)/shard_map/reshape;squeeze;reshape | solution.py:33
  262.6 0.0 copy-start.1
  262.6 0.0 copy-start.3
  262.6 9.3 %fusion.2 = f32[1280,384]{1,0:T(8,128)S(1)} fusion(bf16[1280,4096]{1,0:T(8,128)(2,1)} %reshape_squeeze_reshape.6, bf16[1,4096,384]{2,1,0:T(8,128)(2,1)} %param.9), kind=kOutput, calls=%fused_computation.7 | convolution fusion | flops 4026531840 | bytes 15597568 | tf_op jit(solution)/shard_map/dot_general | solution.py:34
  271.9 0.0 copy-done.1
  271.9 0.0 copy-done.3
  271.9 6.9 %fusion.4 = bf16[1280,384]{1,0:T(8,128)(2,1)} fusion(bf16[1280,4096]{1,0:T(8,128)(2,1)S(1)} %copy-done.1, bf16[1,4096,384]{2,1,0:T(8,128)(2,1)S(1)} %copy-done.3, f32[1280,384]{1,0:T(8,128)S(1)} %fusion.2), kind=kOutput, calls=%fused_computation.9 | convolution fusion | flops 4029480960 | bytes 16580608 | tf_op jit(solution)/shard_map/dot_general | solution.py:35
  278.8 3.0 stack_reshape_reshape_reshape.2
  281.8 1.6 copy.63
  283.4 0.7 stack.4
  284.1 49.1 %all_to_all.31 = bf16[4,4,64,1,5,384]{5,2,4,3,1,0:T(8,128)(2,1)S(1)} all-to-all(bf16[4,4,64,1,5,384]{5,2,4,3,1,0:T(8,128)(2,1)S(1)} %stack.4), channel_id=1, replica_groups=mesh['row'=4,'col'=64] {'row'}, dimensions={0} | all-to-all | bytes 7864320 | tf_op jit(solution)/shard_map/all_to_all | solution.py:42
  333.2 3.0 copy.64
  336.3 0.7 copy.70
  337.0 0.0 copy-done
  337.0 5.5 %convolution_convert_fusion.1 = bf16[1280,1024]{1,0:T(8,128)(2,1)} fusion(bf16[1280,1536]{1,0:T(8,128)(2,1)S(1)} %bitcast.50, bf16[1,1536,1024]{2,1,0:T(8,128)(2,1)S(1)} %copy-done), kind=kOutput, calls=%fused_computation.3 | convolution fusion | flops 4027842560 | bytes 9699328 | tf_op jit(solution)/shard_map/dot_general | solution.py:48
  342.5 6.0 %reshape_transpose_reshape.3 = bf16[4,64,5,1024]{3,2,1,0:T(8,128)(2,1)} reshape(bf16[1280,1024]{1,0:T(8,128)(2,1)} %convolution_convert_fusion.1) | data formatting | bytes 5242880 | tf_op jit(solution)/shard_map/reshape;transpose;reshape | solution.py:53
  348.5 7.3 %copy.65 = bf16[4,64,5,1024]{3,0,2,1:T(4,128)(2,1)S(1)} copy(bf16[4,64,5,1024]{3,2,1,0:T(8,128)(2,1)} %reshape_transpose_reshape.3) | data formatting | bytes 5242880 | tf_op jit(solution)/shard_map/reshape;transpose;reshape | solution.py:53
  355.9 74.4 %all_to_all.32 = bf16[4,64,5,1024]{3,0,2,1:T(4,128)(2,1)S(1)} all-to-all(bf16[4,64,5,1024]{3,0,2,1:T(4,128)(2,1)S(1)} %copy.65), channel_id=1, replica_groups=mesh['row'=4,'col'=64] {'col'}, dimensions={1} | all-to-all | bytes 5242880 | tf_op jit(solution)/shard_map/all_to_all | solution.py:56
  430.2 2.3 copy.66
  432.6 4.7 all-to-all-start.3
  437.3 0.1 copy.68
  437.4 0.1 reshape.50
  437.5 0.0 copy-done.2
  437.6 0.1 copy.56
  437.7 31.4 %all-to-all-done.3 = bf16[4,64,5,1024]{3,1,2,0:T(8,128)(2,1)} async-done(((bf16[4,64,5,1024]{3,1,2,0:T(8,128)(2,1)}), bf16[4,64,5,1024]{3,1,2,0:T(8,128)(2,1)}, u32[]{:S(2)}, u32[]{:S(2)}) %all-to-all-start.3) | async-done | bytes 2621472 | tf_op jit(solution)/shard_map/all_to_all | solution.py:57
  469.1 3.8 copy.67
  472.8 2.6 copy.71
  475.5 7.3 %gather_fusion = bf16[256,4096]{1,0:T(8,128)(2,1)} fusion(bf16[320,4096]{1,0:T(8,128)(2,1)} %bitcast.46, s32[1024]{0:T(1024)S(1)} %pad_clamp_fusion), kind=kCustom, calls=%fused_computation | custom fusion | bytes 4195328 | tf_op jit(solution)/shard_map/gather | solution.py:60
  482.8 5.6 %reshape.60 = f32[128,2,4096]{2,1,0:T(2,128)} reshape(bf16[256,4096]{1,0:T(8,128)(2,1)} %gather_fusion) | data formatting | bytes 6291456 | tf_op jit(solution)/shard_map/convert_element_type | solution.py:60
  488.4 9.6 %multiply_reduce_fusion = bf16[128,4096]{1,0:T(8,128)(2,1)} fusion(f32[128,2,4096]{2,1,0:T(2,128)} %reshape.60, f32[128,2]{1,0:T(8,128)S(1)} %copy.56), kind=kLoop, calls=%fused_computation.2 | loop fusion | flops 1572864 | bytes 5243904 | tf_op jit(solution)/shard_map/reduce_sum | solution.py:61
  (8 shorter events, 0.1 us)
Async XLA Ops:
  6.5 330.4 %copy-start = (bf16[1,1536,1024]{2,1,0:T(8,128)(2,1)S(1)}, bf16[1,1536,1024]{2,1,0:T(8,128)(2,1)}, u32[]{:S(2)}) copy-start(bf16[1,1536,1024]{2,1,0:T(8,128)(2,1)} %param.11) | copy-start | bytes 9437188
  6.5 224.0 %all-gather.3.cloned.1.call-start = ((), (), s32[]{:S(2)}) async-start(), calls=%async_computation.4 | async-start | bytes 13107200 | tf_op jit(solution)/shard_map/all_gather | solution.py:29
  262.6 9.4 %copy-start.1 = (bf16[1280,4096]{1,0:T(8,128)(2,1)S(1)}, bf16[1280,4096]{1,0:T(8,128)(2,1)}, u32[]{:S(2)}) copy-start(bf16[1280,4096]{1,0:T(8,128)(2,1)} %reshape_squeeze_reshape.6) | copy-start | bytes 31457284
  262.6 9.4 %copy-start.3 = (bf16[1,4096,384]{2,1,0:T(8,128)(2,1)S(1)}, bf16[1,4096,384]{2,1,0:T(8,128)(2,1)}, u32[]{:S(2)}) copy-start(bf16[1,4096,384]{2,1,0:T(8,128)(2,1)} %param.10) | copy-start | bytes 9437188
  432.6 4.9 copy-start.2
  432.6 36.5 %all-to-all-start.3 = ((bf16[4,64,5,1024]{3,1,2,0:T(8,128)(2,1)}), bf16[4,64,5,1024]{3,1,2,0:T(8,128)(2,1)}, u32[]{:S(2)}, u32[]{:S(2)}) async-start(bf16[4,64,5,1024]{3,1,2,0:T(8,128)(2,1)} %copy.66), calls=%async_computation.3 | async-start | bytes 5242880 | tf_op jit(solution)/shard_map/all_to_all | solution.py:57
Sparse Core Ops, SparseCore 0:
  129.2 101.2 all-gather.2
